TPU v7x, 32 devices: a whole 2x2x4 slice. The times are simulated.
32 devices in a mesh: dp: 4 (over y, core), seq: 8 (over z, x).
Axes of the slice: x: 2, y: 2, z: 4, core: 2. Of those that a mesh axis runs over, the one named last changes fastest.
Arguments:
- layer_input: bfloat16 [4, 4096, 1024], P('dp', 'seq'), may hold values from -28 to 28
- w_query: bfloat16 [1024, 1024], replicated, may hold values from -0.1875 to 0.1875
- w_key: bfloat16 [1024, 1024], replicated, may hold values from -0.1875 to 0.1875
- w_value: bfloat16 [1024, 1024], replicated, may hold values from -0.1875 to 0.1875
- w_out: bfloat16 [1024, 1024], replicated, may hold values from -0.1875 to 0.1875
- offsets: int32 [3], replicated, may hold values from 0 to 3
- grad_out: bfloat16 [4, 4096, 1024], P('dp', 'seq'), may hold values from -6 to 6
Outputs:
- layer_output: bfloat16 [4, 4096, 1024], P('dp', 'seq')
- grad_x: bfloat16 [4, 4096, 1024], P('dp', 'seq')
- grad_query: float32 [1024, 1024], P('seq')
- grad_key: float32 [1024, 1024], P('seq')
- grad_value: float32 [1024, 1024], P('seq')
- grad_outw: float32 [1024, 1024], P('seq')
All inputs are finite; a program needn't handle non-finite values.
Results may differ from a plain program's by a relative error of at most 0.018.
The roundings to bfloat16 on the way count: a program that leaves them out, or rounds other values in their place, can miss the bound.
Values may be sent and summed in bfloat16 or wider, within the bound.
No kernel may reach another device: no remote copies, remote signals or barrier semaphores. Data moves between devices by JAX's collectives and lax.ppermute only.
A program may use at most 192 MiB of HBM per device.

v0:
```python
import jax
import jax.numpy as jnp
from jax import lax
from jax.sharding import PartitionSpec as P

HEADS = 16
BLOCK = 128


def partner(array, axis, apart):
    return lax.ppermute(array, axis, [(i, i ^ 1 << apart) for i in range(lax.axis_size(axis))])


def swap_blocks(keys_local, values_local, offsets, levels):
    remote = []
    for level in range(levels):
        start = offsets[level] * BLOCK
        pair = jnp.stack(
            [
                lax.dynamic_slice_in_dim(keys_local, start, BLOCK, 0),
                lax.dynamic_slice_in_dim(values_local, start, BLOCK, 0),
            ]
        )
        remote.append(partner(pair, "seq", level))
    return remote


def gradient_terms(sources):
    parts = []
    for left, right in sources:
        parts.append(jnp.dot(left.T, right, preferred_element_type=jnp.float32))
    return jnp.concatenate(parts, axis=1)


def body(layer_input, w_query, w_key, w_value, w_out, offsets, grad_out):
    rows = layer_input[0]
    cot = grad_out[0]
    tok = rows.shape[0]
    width = rows.shape[1]
    head = width // HEADS
    scale = head ** (-0.5)
    levels = lax.axis_size("seq").bit_length() - 1
    query = jnp.dot(rows, w_query, preferred_element_type=jnp.float32).astype(jnp.bfloat16)
    keys_local = jnp.dot(rows, w_key, preferred_element_type=jnp.float32).astype(jnp.bfloat16)
    values_local = jnp.dot(rows, w_value, preferred_element_type=jnp.float32).astype(jnp.bfloat16)
    remote = swap_blocks(keys_local, values_local, offsets, levels)
    all_keys = jnp.concatenate([keys_local] + [piece[0] for piece in remote], 0)
    all_values = jnp.concatenate([values_local] + [piece[1] for piece in remote], 0)
    total_keys = all_keys.shape[0]
    group = min(tok, 512)
    count = tok // group

    def split3(a):
        return a.reshape(a.shape[0], HEADS, head)

    def forward(query_group):
        scores = (
            jnp.einsum(
                "qhe,khe->hqk",
                split3(query_group),
                split3(all_keys),
                preferred_element_type=jnp.float32,
            )
            * scale
        )
        top = jnp.max(scores, axis=-1, keepdims=True)
        lse = top + jnp.log(jnp.sum(jnp.exp(scores - top), axis=-1, keepdims=True))
        prob_b = jnp.exp(scores - lse).astype(jnp.bfloat16)
        attended = jnp.einsum(
            "hqk,khe->qhe", prob_b, split3(all_values), preferred_element_type=jnp.float32
        )
        return (attended.reshape(group, width).astype(jnp.bfloat16), lse)

    query_groups = query.reshape(count, group, width)
    att_groups, lses = lax.map(forward, query_groups)
    attended = att_groups.reshape(tok, width)
    result = jnp.dot(attended, w_out, preferred_element_type=jnp.float32).astype(jnp.bfloat16)
    d_att = jnp.dot(cot, w_out.T, preferred_element_type=jnp.float32).astype(jnp.bfloat16)

    def backward(carry, item):
        query_group, dgroup, lse = item
        scores = (
            jnp.einsum(
                "qhe,khe->hqk",
                split3(query_group),
                split3(all_keys),
                preferred_element_type=jnp.float32,
            )
            * scale
        )
        prob = jnp.exp(scores - lse)
        prob_b = prob.astype(jnp.bfloat16)
        dprob = jnp.einsum(
            "qhe,khe->hqk", split3(dgroup), split3(all_values), preferred_element_type=jnp.float32
        )
        delta = jnp.sum(prob * dprob, axis=-1, keepdims=True)
        dscore = (prob * (dprob - delta) * scale).astype(jnp.bfloat16)
        dquery = jnp.einsum(
            "hqk,khe->qhe", dscore, split3(all_keys), preferred_element_type=jnp.float32
        )
        dkeys = jnp.einsum(
            "hqk,qhe->khe", dscore, split3(query_group), preferred_element_type=jnp.float32
        )
        dvalues = jnp.einsum(
            "hqk,qhe->khe", prob_b, split3(dgroup), preferred_element_type=jnp.float32
        )
        new_carry = (
            carry[0] + dkeys.reshape(total_keys, width),
            carry[1] + dvalues.reshape(total_keys, width),
        )
        return (new_carry, dquery.reshape(group, width).astype(jnp.bfloat16))

    empty = jnp.zeros((total_keys, width), jnp.float32)
    (dk_acc, dv_acc), dq_groups = lax.scan(
        backward, (empty, empty), (query_groups, d_att.reshape(count, group, width), lses)
    )
    dquery = dq_groups.reshape(tok, width)
    dkey_sum = dk_acc[:tok]
    dvalue_sum = dv_acc[:tok]
    for level in range(levels):
        low = tok + level * BLOCK
        piece = jnp.stack([dk_acc[low : low + BLOCK], dv_acc[low : low + BLOCK]])
        returned = partner(piece.astype(jnp.bfloat16), "seq", level).astype(piece.dtype)
        start = offsets[level] * BLOCK
        dkey_sum = lax.dynamic_update_slice_in_dim(
            dkey_sum, lax.dynamic_slice_in_dim(dkey_sum, start, BLOCK, 0) + returned[0], start, 0
        )
        dvalue_sum = lax.dynamic_update_slice_in_dim(
            dvalue_sum,
            lax.dynamic_slice_in_dim(dvalue_sum, start, BLOCK, 0) + returned[1],
            start,
            0,
        )
    dkey = dkey_sum.astype(jnp.bfloat16)
    dvalue = dvalue_sum.astype(jnp.bfloat16)
    total = jnp.dot(dquery, w_query.T, preferred_element_type=jnp.float32)
    total = total + jnp.dot(dkey, w_key.T, preferred_element_type=jnp.float32)
    total = total + jnp.dot(dvalue, w_value.T, preferred_element_type=jnp.float32)
    grad_input = total.astype(jnp.bfloat16)
    sources = ((rows, dquery), (rows, dkey), (rows, dvalue), (attended, cot))
    part = lax.psum_scatter(
        gradient_terms(sources).astype(jnp.bfloat16), "seq", scatter_dimension=0, tiled=True
    )
    summed = lax.psum(part, "dp").astype(jnp.float32)
    return (
        result[None],
        grad_input[None],
        summed[:, :width],
        summed[:, width : 2 * width],
        summed[:, 2 * width : 3 * width],
        summed[:, 3 * width :],
    )


def solution(mesh):
    return jax.shard_map(
        body,
        mesh=mesh,
        in_specs=(P("dp", "seq", None), P(), P(), P(), P(), P(), P("dp", "seq", None)),
        out_specs=(
            P("dp", "seq", None),
            P("dp", "seq", None),
            P("seq", None),
            P("seq", None),
            P("seq", None),
            P("seq", None),
        ),
        check_vma=False,
    )
```

profile of v0, /device:TPU:0, one launch (start us, length us, event | category | flops | bytes accessed | tf_op | source)
XLA Modules:
  0.0 489.7 jit_solution(11821833035171614596)
XLA Ops:
  10.6 3.3 convolution_convert_fusion.4
  18.5 3.0 collective-permute-start.1
  22.3 2.6 collective-permute-start.2
  29.5 2.3 convolution_convert_fusion.1
  31.8 2.8 copy.37
  39.7 4.3 collective-permute-done.1
  59.7 15.5 %multiply_reduce_fusion.1 = (f32[16,512]{1,0:T(8,128)S(1)}, f32[16,512,896]{2,1,0:T(8,128)}) fusion(bf16[512,16,64]{0,2,1:T(8,128)(2,1)} %bitcast.130, bf16[128,16,64]{0,2,1:T(8,128)(2,1)} %bitcast.144, bf16[128,16,64]{0,2,1:T(8,128)(2,1)} %bitcast.142, bf16[128,16,64]{0,2,1:T(8,128)(2,1)} %bitcast.146, bf16[512,16,64]{0,2,1:T(8,128)(2,1)} %bitcast.132), kind=kOutput, calls=%fused_computation.6 | convolution fusion | flops 961536000 | bytes 32276480 | tf_op jit(solution)/shard_map/while/body/eval_jaxpr/qhe,khe->hqk/dot_general | solution.py:58
  75.1 13.1 %exponential_reduce_fusion = f32[16,512]{1,0:T(8,128)S(1)} fusion(f32[16,512,896]{2,1,0:T(8,128)} %get-tuple-element.101, f32[16,512]{1,0:T(8,128)S(1)} %get-tuple-element.100), kind=kLoop, calls=%fused_computation.5 | loop fusion | flops 22011904 | bytes 29425664 | tf_op jit(solution)/shard_map/while/body/eval_jaxpr/reduce_sum | solution.py:67
  88.3 11.6 %fusion.60 = f32[16,512,896]{2,1,0:T(8,128)} fusion(bf16[512,16,64]{0,2,1:T(8,128)(2,1)S(1)} %bitcast.125, bf16[128,16,64]{0,2,1:T(8,128)(2,1)S(1)} %bitcast.139, bf16[128,16,64]{0,2,1:T(8,128)(2,1)S(1)} %bitcast.136, bf16[128,16,64]{0,2,1:T(8,128)(2,1)S(1)} %bitcast.141, bf16[512,16,64]{0,2,1:T(8,128)(2,1)S(1)} %bitcast.128), kind=kOutput, calls=%fused_computation.72 | convolution fusion | flops 946864128 | bytes 32243712 | tf_op jit(solution)/shard_map/while/body/eval_jaxpr/qhe,khe->hqk/dot_general | solution.py:93
  100.0 60.6 %fusion.29 = bf16[16,64,512]{2,1,0:T(8,128)(2,1)} fusion(f32[16,512,896]{2,1,0:T(8,128)} %fusion.60, f32[16,512,896]{2,1,0:T(8,128)} %get-tuple-element.101, f32[16,512]{1,0:T(8,128)S(1)} %log_add_fusion, bf16[128,16,64]{0,2,1:T(8,128)(2,1)} %bitcast.145, bf16[128,16,64]{0,2,1:T(8,128)(2,1)} %bitcast.143, bf16[128,16,64]{0,2,1:T(8,128)(2,1)} %bitcast.147, ...), kind=kOutput, calls=%fused_computation.31 | convolution fusion | flops 1013457792 | bytes 61636608 | tf_op jit(solution)/shard_map/while/body/eval_jaxpr/hqk,khe->qhe/dot_general | solution.py:98
  160.6 54.9 %fusion.81 = (bf16[896,16,64]{0,2,1:T(8,128)(2,1)}, f32[896,16,64]{0,2,1:T(8,128)}) fusion(bf16[512,16,64]{0,2,1:T(8,128)(2,1)} %bitcast.131, f32[16,512,896]{2,1,0:T(8,128)} %fusion.60, f32[16,512,896]{2,1,0:T(8,128)} %get-tuple-element.101, f32[16,512]{1,0:T(8,128)S(1)} %log_add_fusion), kind=kOutput, calls=%fused_computation.98 | convolution fusion | flops 1006510976 | bytes 65306624 | tf_op jit(solution)/shard_map/while/body/eval_jaxpr/hqk,qhe->khe/dot_general | solution.py:101
  215.5 13.6 %fusion.26 = bf16[16,64,512]{2,1,0:T(8,128)(2,1)} fusion(f32[16,512,896]{2,1,0:T(8,128)} %get-tuple-element.101, f32[16,512]{1,0:T(8,128)S(1)} %log_add_fusion, bf16[128,16,64]{0,2,1:T(8,128)(2,1)} %bitcast.138, bf16[128,16,64]{0,2,1:T(8,128)(2,1)S(1)} %bitcast.137, bf16[128,16,64]{0,2,1:T(8,128)(2,1)} %bitcast.140, bf16[512,16,64]{0,2,1:T(8,128)(2,1)} %bitcast.127), kind=kOutput, calls=%fused_computation.25 | convolution fusion | flops 969408512 | bytes 32276480 | tf_op jit(solution)/shard_map/while/body/eval_jaxpr/hqk,khe->qhe/dot_general | solution.py:69
  229.1 11.7 %fusion.80 = (bf16[896,16,64]{0,2,1:T(8,128)(2,1)S(1)}, f32[896,16,64]{0,2,1:T(8,128)S(1)}) fusion(bf16[512,16,64]{0,2,1:T(8,128)(2,1)S(1)} %bitcast.126, f32[16,512,896]{2,1,0:T(8,128)} %get-tuple-element.101, f32[16,512]{1,0:T(8,128)S(1)} %log_add_fusion), kind=kOutput, calls=%fused_computation.97 | convolution fusion | flops 962461696 | bytes 35946496 | tf_op jit(solution)/shard_map/while/body/eval_jaxpr/hqk,qhe->khe/dot_general | solution.py:104
  244.4 3.1 collective-permute-start.5
  251.9 3.8 collective-permute-done.3
  255.7 12.0 %collective-permute-done.4 = bf16[2,128,1024]{1,2,0:T(8,128)(2,1)S(1)} collective-permute-done((bf16[2,128,1024]{1,2,0:T(8,128)(2,1)S(1)}, bf16[2,128,1024]{1,2,0:T(8,128)(2,1)S(1)}, u32[]{:S(2)}, u32[]{:S(2)}) %collective-permute-start.4) | collective-permute-done | bytes 524320 | tf_op jit(solution)/shard_map/ppermute | solution.py:11
  272.9 4.0 pad_maximum_fusion
  276.9 11.5 %copy.51 = bf16[1024,4096]{1,0:T(8,128)(2,1)} copy(bf16[1024,4096]{0,1:T(8,128)(2,1)} %pad_maximum_fusion) | data formatting | bytes 16777216
  290.8 2.7 fusion.84
  293.5 2.7 fusion.57
  296.2 140.5 %reduce-scatter.4.cloned.1.call-done = bf16[128,4096]{1,0:T(8,128)(2,1)} async-done(((bf16[1024,4096]{1,0:T(8,128)(2,1)}), bf16[128,4096]{1,0:T(8,128)(2,1)}) %reduce-scatter.4.cloned.1.call-update) | async-done | bytes 1048592
  439.0 5.8 %fusion.33 = bf16[1,512,1024]{2,1,0:T(8,128)(2,1)} fusion(bf16[1024,1024]{1,0:T(8,128)(2,1)} %param.10, f32[512,1024]{1,0:T(8,128)} %fusion.84, f32[512,1024]{1,0:T(8,128)} %fusion.57, f32[512,1024]{0,1:T(8,128)} %copy-done.1), kind=kOutput, calls=%fused_computation.33 | convolution fusion | flops 1075838976 | bytes 9437184 | tf_op jit(solution)/shard_map/dot_general | solution.py:138
  444.8 29.6 %all-reduce.2.cloned.1.call-done = bf16[128,4096]{0,1:T(8,128)(2,1)} async-done(((bf16[128,4096]{0,1:T(8,128)(2,1)}), bf16[128,4096]{0,1:T(8,128)(2,1)}) %all-reduce.2.cloned.1.call-update) | async-done | bytes 1048592 | tf_op jit(solution)/shard_map/psum | solution.py:144
  474.3 2.3 fusion.75
  (93 shorter events, 55.9 us)
Async XLA Ops:
  7.2 22.3 %copy-start = (bf16[1024,1024]{1,0:T(8,128)(2,1)S(1)}, bf16[1024,1024]{1,0:T(8,128)(2,1)}, u32[]{:S(2)}) copy-start(bf16[1024,1024]{1,0:T(8,128)(2,1)} %param.11) | copy-start | bytes 6291460
  7.2 429.5 %reduce-scatter.4.cloned.1.call-start = ((), (), s32[]{:S(2)}) async-start(), calls=%async_computation.2 | async-start | bytes 9437184
  10.6 3.3 copy-start.8
  10.6 3.3 copy-start.15
  16.2 11.1 %copy-start.10 = (bf16[1024,1024]{1,0:T(8,128)(2,1)S(1)}, bf16[1024,1024]{1,0:T(8,128)(2,1)}, u32[]{:S(2)}) copy-start(bf16[1024,1024]{1,0:T(8,128)(2,1)} %param.8) | copy-start | bytes 6291460
  16.2 11.1 %copy-start.16 = (bf16[1,512,1024]{2,1,0:T(8,128)(2,1)S(1)}, bf16[1,512,1024]{2,1,0:T(8,128)(2,1)}, u32[]{:S(2)}) copy-start(bf16[1,512,1024]{2,1,0:T(8,128)(2,1)} %param.7) | copy-start | bytes 3145732
  18.5 25.5 %collective-permute-start.1 = (bf16[2,128,1024]{2,1,0:T(8,128)(2,1)}, bf16[2,128,1024]{2,1,0:T(8,128)(2,1)}, u32[]{:S(2)}, u32[]{:S(2)}) collective-permute-start(bf16[2,128,1024]{2,1,0:T(8,128)(2,1)} %pad_maximum_fusion.4), channel_id=1, source_target_pairs={{0,2},{1,3},{2,0},{3,1},{4,6},{5,7},{6,4},{7,5},{8,10},{9,11},{10,... | collective-permute-start | bytes 1572872 | tf_op jit(solution)/shard_map/ppermute | solution.py:11
  22.3 26.5 %collective-permute-start.2 = (bf16[2,128,1024]{2,1,0:T(8,128)(2,1)}, bf16[2,128,1024]{2,1,0:T(8,128)(2,1)}, u32[]{:S(2)}, u32[]{:S(2)}) collective-permute-start(bf16[2,128,1024]{2,1,0:T(8,128)(2,1)} %pad_maximum_fusion.5), channel_id=1, source_target_pairs={{0,4},{1,5},{2,6},{3,7},{4,0},{5,1},{6,2},{7,3},{8,12},{9,13},{10,... | collective-permute-start | bytes 1572872 | tf_op jit(solution)/shard_map/ppermute | solution.py:11
  25.8 3.7 copy-start.13
  25.8 28.5 %collective-permute-start = (bf16[2,128,1024]{2,1,0:T(8,128)(2,1)}, bf16[2,128,1024]{2,1,0:T(8,128)(2,1)}, u32[]{:S(2)}, u32[]{:S(2)}) collective-permute-start(bf16[2,128,1024]{2,1,0:T(8,128)(2,1)} %pad_maximum_fusion.3), channel_id=1, source_target_pairs={{0,1},{1,0},{2,3},{3,2},{4,5},{5,4},{6,7},{7,6},{8,9},{9,8},{10,11... | collective-permute-start | bytes 1572872 | tf_op jit(solution)/shard_map/ppermute | solution.py:11
  75.1 13.2 %copy-start.2 = (bf16[512,1024]{0,1:T(8,128)(2,1)S(1)}, bf16[512,1024]{0,1:T(8,128)(2,1)}, u32[]{:S(2)}) copy-start(bf16[512,1024]{0,1:T(8,128)(2,1)} %copy.37) | copy-start | bytes 3145732
  75.1 13.2 %copy-start.6 = (bf16[1,128,1024]{1,2,0:T(8,128)(2,1)S(1)}, bf16[1,128,1024]{1,2,0:T(8,128)(2,1)}, u32[]{:S(2)}) copy-start(bf16[1,128,1024]{1,2,0:T(8,128)(2,1)} %copy.40) | copy-start | bytes 786436
  75.1 13.2 %copy-start.7 = (bf16[1,128,1024]{1,2,0:T(8,128)(2,1)S(1)}, bf16[1,128,1024]{1,2,0:T(8,128)(2,1)}, u32[]{:S(2)}) copy-start(bf16[1,128,1024]{1,2,0:T(8,128)(2,1)} %copy.38) | copy-start | bytes 786436
  240.9 6.6 %copy-start.9 = (f32[896,16,64]{0,2,1:T(8,128)S(1)}, f32[896,16,64]{0,2,1:T(8,128)}, u32[]{:S(2)}) copy-start(f32[896,16,64]{0,2,1:T(8,128)} %get-tuple-element.105) | copy-start | bytes 11010052
  242.5 13.2 %collective-permute-start.3 = (bf16[2,128,1024]{1,2,0:T(8,128)(2,1)S(1)}, bf16[2,128,1024]{1,2,0:T(8,128)(2,1)S(1)}, u32[]{:S(2)}, u32[]{:S(2)}) collective-permute-start(bf16[2,128,1024]{1,2,0:T(8,128)(2,1)S(1)} %pad_maximum_fusion.6), channel_id=1, source_target_pairs={{0,1},{1,0},{2,3},{3,2},{4,5},{5,4},{6,7},{7,6},{8,9},{9,8},{10,11... | collective-permute-start | bytes 1572872 | tf_op jit(solution)/shard_map/ppermute | solution.py:11
  244.3 23.5 %collective-permute-start.4 = (bf16[2,128,1024]{1,2,0:T(8,128)(2,1)S(1)}, bf16[2,128,1024]{1,2,0:T(8,128)(2,1)S(1)}, u32[]{:S(2)}, u32[]{:S(2)}) collective-permute-start(bf16[2,128,1024]{1,2,0:T(8,128)(2,1)S(1)} %pad_maximum_fusion.7), channel_id=1, source_target_pairs={{0,2},{1,3},{2,0},{3,1},{4,6},{5,7},{6,4},{7,5},{8,10},{9,11},{10,... | collective-permute-start | bytes 1572872 | tf_op jit(solution)/shard_map/ppermute | solution.py:11
  244.4 24.9 %collective-permute-start.5 = (bf16[2,128,1024]{1,2,0:T(8,128)(2,1)S(1)}, bf16[2,128,1024]{1,2,0:T(8,128)(2,1)S(1)}, u32[]{:S(2)}, u32[]{:S(2)}) collective-permute-start(bf16[2,128,1024]{1,2,0:T(8,128)(2,1)S(1)} %pad_maximum_fusion.8), channel_id=1, source_target_pairs={{0,4},{1,5},{2,6},{3,7},{4,0},{5,1},{6,2},{7,3},{8,12},{9,13},{10,... | collective-permute-start | bytes 1572872 | tf_op jit(solution)/shard_map/ppermute | solution.py:11
  247.5 1.6 copy-start.14
  269.7 1.9 copy-start.3
  288.5 185.9 %all-reduce.2.cloned.1.call-start = ((), (), s32[]{:S(2)}) async-start(), calls=%async_computation.1 | async-start | bytes 2097152 | tf_op jit(solution)/shard_map/psum | solution.py:144
  288.5 2.3 copy-start.11
  288.5 2.3 copy-start.19
  290.8 2.7 copy-start.4
  290.8 2.7 copy-start.12
  (4 other events, 5.4 us)
Sparse Core Ops, SparseCore 0:
  288.6 148.0 reduce-scatter.3
  439.2 35.1 all-reduce.1
where the time goes:
time: 495 us; the launch traced here: 490 us
  matrix products  197 us (40%)
  waiting for transfers between devices  191 us (39%)
  local copies, waits for them, and re-layouts  52.5 us (11%)
  other arithmetic  21 us (4%)
  between operations  16.5 us (3%)
  starting transfers between devices  12.1 us (2%)
    unnamed x3, waiting for transfers between devices  141 us
    dot_general x1, matrix products, backward(): jnp.einsum('hqk,khe->qhe', dscore, split3(all_keys), preferred_element_ty...  60.6 us
    dot_general x1, matrix products, backward(): jnp.einsum('hqk,qhe->khe', dscore, split3(query_group), preferred_element...  54.9 us
    psum x1, waiting for transfers between devices, body(): summed = lax.psum(part, 'dp').astype(jnp.float32)  29.6 us
    unnamed x46, local copies, waits for them, and re-layouts  21.9 us
    ppermute x6, waiting for transfers between devices, partner(): lax.ppermute(array, axis, [(i, i ^ 1 << apart) for i in range(lax.axis_si...  20.9 us
    dot_general x1, matrix products, forward(): jnp.einsum('qhe,khe->hqk', split3(query_group), split3(all_keys), preferr...  15.5 us
    dot_general x1, matrix products, forward(): jnp.einsum('hqk,khe->qhe', prob_b, split3(all_values), preferred_element_...  13.6 us
  transfers between devices with their start and end apart: 8, of which 6 were waited for; matrix products, arithmetic and copies ran while one was open for 8% of the time, Pallas kernels for 0%

commit v1 on v0

--- a/solution.py
+++ b/solution.py
@@ -141,7 +141,7 @@
     part = lax.psum_scatter(
         gradient_terms(sources).astype(jnp.bfloat16), "seq", scatter_dimension=0, tiled=True
     )
-    summed = lax.psum(part, "dp").astype(jnp.float32)
+    summed = jnp.sum(lax.all_gather(part, "dp"), axis=0).astype(jnp.float32)
     return (
         result[None],
         grad_input[None],

time: 495 us -> 525 us (1.061)
  other arithmetic: 21 us -> 44 us
  local copies, waits for them, and re-layouts: 52.5 us -> 62.8 us
  matrix products: 197 us -> 191 us
    psum x1 -> x0, waiting for transfers between devices: 29.6 us -> none  [body(): summed = lax.psum(part, 'dp').astype(jnp.float32)]
    all_gather x0 -> x1, waiting for transfers between devices: none -> 24.7 us  [body(): summed = jnp.sum(lax.all_gather(part, 'dp'), axis=0).astype(jnp.float32)]
    reduce_sum x0 -> x1, other arithmetic: none -> 23 us  [body(): summed = jnp.sum(lax.all_gather(part, 'dp'), axis=0).astype(jnp.float32)]
    unnamed x3, waiting for transfers between devices: 141 us -> 148 us
    all_gather x0 -> x1, local copies, waits for them, and re-layouts: none -> 6.97 us  [body(): summed = jnp.sum(lax.all_gather(part, 'dp'), axis=0).astype(jnp.float32)]
    unnamed x46 -> x50, local copies, waits for them, and re-layouts: 21.9 us -> 26.3 us
  transfers between devices with their start and end apart: 8 -> 8, of which waited for: 6 -> 6; matrix products, arithmetic and copies ran while one was open for 8% -> 7% of each run, Pallas kernels for 0% -> 0%
where the time goes in v1:
time: 525 us; the launch traced here: 520 us
  waiting for transfers between devices  194 us (37%)
  matrix products  191 us (36%)
  local copies, waits for them, and re-layouts  62.8 us (12%)
  other arithmetic  44 us (8%)
  between operations  16.6 us (3%)
  starting transfers between devices  12.1 us (2%)
    unnamed x3, waiting for transfers between devices  148 us
    dot_general x1, matrix products, backward(): jnp.einsum('hqk,khe->qhe', dscore, split3(all_keys), preferred_element_ty...  60.9 us
    dot_general x1, matrix products, backward(): jnp.einsum('hqk,qhe->khe', dscore, split3(query_group), preferred_element...  55 us
    unnamed x50, local copies, waits for them, and re-layouts  26.3 us
    all_gather x1, waiting for transfers between devices, body(): summed = jnp.sum(lax.all_gather(part, 'dp'), axis=0).astype(jnp.float32)  24.7 us
    reduce_sum x1, other arithmetic, body(): summed = jnp.sum(lax.all_gather(part, 'dp'), axis=0).astype(jnp.float32)  23 us
    ppermute x6, waiting for transfers between devices, partner(): lax.ppermute(array, axis, [(i, i ^ 1 << apart) for i in range(lax.axis_si...  21.1 us
    dot_general x1, matrix products, forward(): jnp.einsum('qhe,khe->hqk', split3(query_group), split3(all_keys), preferr...  15.5 us
  transfers between devices with their start and end apart: 8, of which 6 were waited for; matrix products, arithmetic and copies ran while one was open for 7% of the time, Pallas kernels for 0%

profile of v1, /device:TPU:0, one launch (start us, length us, event | category | flops | bytes accessed | tf_op | source)
XLA Modules:
  0.0 520.2 jit_solution(4515256450750933415)
XLA Ops:
  10.6 3.3 convolution_convert_fusion.4
  18.5 3.0 collective-permute-start.1
  22.3 2.6 collective-permute-start.2
  29.5 2.3 convolution_convert_fusion.1
  31.8 2.6 copy.29
  39.5 4.5 collective-permute-done.1
  59.6 15.5 %multiply_reduce_fusion.1 = (f32[16,512]{1,0:T(8,128)S(1)}, f32[16,512,896]{2,1,0:T(8,128)}) fusion(bf16[512,16,64]{0,2,1:T(8,128)(2,1)} %bitcast.132, bf16[128,16,64]{0,2,1:T(8,128)(2,1)} %bitcast.146, bf16[128,16,64]{0,2,1:T(8,128)(2,1)} %bitcast.144, bf16[128,16,64]{0,2,1:T(8,128)(2,1)} %bitcast.148, bf16[512,16,64]{0,2,1:T(8,128)(2,1)} %bitcast.134), kind=kOutput, calls=%fused_computation.6 | convolution fusion | flops 961536000 | bytes 32276480 | tf_op jit(solution)/shard_map/while/body/eval_jaxpr/qhe,khe->hqk/dot_general | solution.py:58
  75.1 13.1 %exponential_reduce_fusion = f32[16,512]{1,0:T(8,128)S(1)} fusion(f32[16,512,896]{2,1,0:T(8,128)} %get-tuple-element.89, f32[16,512]{1,0:T(8,128)S(1)} %get-tuple-element.88), kind=kLoop, calls=%fused_computation.5 | loop fusion | flops 22011904 | bytes 29425664 | tf_op jit(solution)/shard_map/while/body/eval_jaxpr/reduce_sum | solution.py:67
  88.3 11.6 %fusion.60 = f32[16,512,896]{2,1,0:T(8,128)} fusion(bf16[512,16,64]{0,2,1:T(8,128)(2,1)S(1)} %bitcast.127, bf16[128,16,64]{0,2,1:T(8,128)(2,1)S(1)} %bitcast.141, bf16[128,16,64]{0,2,1:T(8,128)(2,1)S(1)} %bitcast.138, bf16[128,16,64]{0,2,1:T(8,128)(2,1)S(1)} %bitcast.143, bf16[512,16,64]{0,2,1:T(8,128)(2,1)S(1)} %bitcast.130), kind=kOutput, calls=%fused_computation.72 | convolution fusion | flops 946864128 | bytes 32243712 | tf_op jit(solution)/shard_map/while/body/eval_jaxpr/qhe,khe->hqk/dot_general | solution.py:93
  100.0 60.9 %fusion.29 = bf16[16,64,512]{2,1,0:T(8,128)(2,1)} fusion(f32[16,512,896]{2,1,0:T(8,128)} %fusion.60, f32[16,512,896]{2,1,0:T(8,128)} %get-tuple-element.89, f32[16,512]{1,0:T(8,128)S(1)} %log_add_fusion, bf16[128,16,64]{0,2,1:T(8,128)(2,1)} %bitcast.147, bf16[128,16,64]{0,2,1:T(8,128)(2,1)} %bitcast.145, bf16[128,16,64]{0,2,1:T(8,128)(2,1)} %bitcast.149, ...), kind=kOutput, calls=%fused_computation.31 | convolution fusion | flops 1013457792 | bytes 61636608 | tf_op jit(solution)/shard_map/while/body/eval_jaxpr/hqk,khe->qhe/dot_general | solution.py:98
  160.9 55.0 %fusion.81 = (bf16[896,16,64]{0,2,1:T(8,128)(2,1)}, f32[896,16,64]{0,2,1:T(8,128)}) fusion(bf16[512,16,64]{0,2,1:T(8,128)(2,1)} %bitcast.133, f32[16,512,896]{2,1,0:T(8,128)} %fusion.60, f32[16,512,896]{2,1,0:T(8,128)} %get-tuple-element.89, f32[16,512]{1,0:T(8,128)S(1)} %log_add_fusion), kind=kOutput, calls=%fused_computation.98 | convolution fusion | flops 1006510976 | bytes 65306624 | tf_op jit(solution)/shard_map/while/body/eval_jaxpr/hqk,qhe->khe/dot_general | solution.py:101
  216.0 13.6 %fusion.26 = bf16[16,64,512]{2,1,0:T(8,128)(2,1)} fusion(f32[16,512,896]{2,1,0:T(8,128)} %get-tuple-element.89, f32[16,512]{1,0:T(8,128)S(1)} %log_add_fusion, bf16[128,16,64]{0,2,1:T(8,128)(2,1)} %bitcast.140, bf16[128,16,64]{0,2,1:T(8,128)(2,1)S(1)} %bitcast.139, bf16[128,16,64]{0,2,1:T(8,128)(2,1)} %bitcast.142, bf16[512,16,64]{0,2,1:T(8,128)(2,1)} %bitcast.129), kind=kOutput, calls=%fused_computation.25 | convolution fusion | flops 969408512 | bytes 32276480 | tf_op jit(solution)/shard_map/while/body/eval_jaxpr/hqk,khe->qhe/dot_general | solution.py:69
  229.6 11.7 %fusion.80 = (bf16[896,16,64]{0,2,1:T(8,128)(2,1)S(1)}, f32[896,16,64]{0,2,1:T(8,128)S(1)}) fusion(bf16[512,16,64]{0,2,1:T(8,128)(2,1)S(1)} %bitcast.128, f32[16,512,896]{2,1,0:T(8,128)} %get-tuple-element.89, f32[16,512]{1,0:T(8,128)S(1)} %log_add_fusion), kind=kOutput, calls=%fused_computation.97 | convolution fusion | flops 962461696 | bytes 35946496 | tf_op jit(solution)/shard_map/while/body/eval_jaxpr/hqk,qhe->khe/dot_general | solution.py:104
  244.8 3.1 collective-permute-start.5
  252.3 3.8 collective-permute-done.3
  256.2 12.0 %collective-permute-done.4 = bf16[2,128,1024]{1,2,0:T(8,128)(2,1)S(1)} collective-permute-done((bf16[2,128,1024]{1,2,0:T(8,128)(2,1)S(1)}, bf16[2,128,1024]{1,2,0:T(8,128)(2,1)S(1)}, u32[]{:S(2)}, u32[]{:S(2)}) %collective-permute-start.4) | collective-permute-done | bytes 524320 | tf_op jit(solution)/shard_map/ppermute | solution.py:11
  273.3 4.0 pad_maximum_fusion
  277.4 11.4 %copy.43 = bf16[1024,4096]{1,0:T(8,128)(2,1)} copy(bf16[1024,4096]{0,1:T(8,128)(2,1)} %pad_maximum_fusion) | data formatting | bytes 16777216
  288.8 148.2 %reduce-scatter.4.cloned.1.call-done = bf16[128,4096]{1,0:T(8,128)(2,1)} async-done(((bf16[1024,4096]{1,0:T(8,128)(2,1)}), bf16[128,4096]{1,0:T(8,128)(2,1)}) %reduce-scatter.4.cloned.1.call-update) | async-done | bytes 1048592
  437.1 2.5 copy.44
  446.7 2.3 fusion.33
  449.0 24.7 %all-gather.3.cloned.1.call-done = bf16[512,4096]{0,1:T(8,128)(2,1)} async-done(((bf16[128,4096]{0,1:T(8,128)(2,1)}), bf16[512,4096]{0,1:T(8,128)(2,1)}) %all-gather.3.cloned.1.call-update) | async-done | bytes 4194320 | tf_op jit(solution)/shard_map/all_gather | solution.py:144
  473.7 7.0 %reshape.105 = bf16[4,128,4096]{1,0,2:T(4,128)(2,1)} reshape(bf16[512,4096]{0,1:T(8,128)(2,1)} %all-gather.3.cloned.1.call-done) | data formatting | bytes 8388608 | tf_op jit(solution)/shard_map/all_gather | solution.py:144
  480.7 23.0 %reduce_sum.34 = bf16[128,4096]{0,1:T(8,128)(2,1)S(1)} reduce(bf16[4,128,4096]{1,0,2:T(4,128)(2,1)} %reshape.105, bf16[]{:T(256)} %constant.46.clone.1), dimensions={0}, to_apply=%region_4.5 | reduce | flops 1572864 | bytes 5242882 | tf_op jit(solution)/shard_map/reduce_sum | solution.py:144
  (99 shorter events, 61.9 us)
Async XLA Ops:
  7.2 22.3 %copy-start = (bf16[1024,1024]{1,0:T(8,128)(2,1)S(1)}, bf16[1024,1024]{1,0:T(8,128)(2,1)}, u32[]{:S(2)}) copy-start(bf16[1024,1024]{1,0:T(8,128)(2,1)} %param.11) | copy-start | bytes 6291460
  7.2 429.9 %reduce-scatter.4.cloned.1.call-start = ((), (), s32[]{:S(2)}) async-start(), calls=%async_computation.2 | async-start | bytes 9437184
  10.6 3.3 copy-start.9
  10.6 3.3 copy-start.17
  16.2 11.1 %copy-start.12 = (bf16[1024,1024]{1,0:T(8,128)(2,1)S(1)}, bf16[1024,1024]{1,0:T(8,128)(2,1)}, u32[]{:S(2)}) copy-start(bf16[1024,1024]{1,0:T(8,128)(2,1)} %param.8) | copy-start | bytes 6291460
  16.2 11.1 %copy-start.18 = (bf16[1,512,1024]{2,1,0:T(8,128)(2,1)S(1)}, bf16[1,512,1024]{2,1,0:T(8,128)(2,1)}, u32[]{:S(2)}) copy-start(bf16[1,512,1024]{2,1,0:T(8,128)(2,1)} %param.7) | copy-start | bytes 3145732
  18.5 25.5 %collective-permute-start.1 = (bf16[2,128,1024]{2,1,0:T(8,128)(2,1)}, bf16[2,128,1024]{2,1,0:T(8,128)(2,1)}, u32[]{:S(2)}, u32[]{:S(2)}) collective-permute-start(bf16[2,128,1024]{2,1,0:T(8,128)(2,1)} %pad_maximum_fusion.4), channel_id=1, source_target_pairs={{0,2},{1,3},{2,0},{3,1},{4,6},{5,7},{6,4},{7,5},{8,10},{9,11},{10,... | collective-permute-start | bytes 1572872 | tf_op jit(solution)/shard_map/ppermute | solution.py:11
  22.3 26.5 %collective-permute-start.2 = (bf16[2,128,1024]{2,1,0:T(8,128)(2,1)}, bf16[2,128,1024]{2,1,0:T(8,128)(2,1)}, u32[]{:S(2)}, u32[]{:S(2)}) collective-permute-start(bf16[2,128,1024]{2,1,0:T(8,128)(2,1)} %pad_maximum_fusion.5), channel_id=1, source_target_pairs={{0,4},{1,5},{2,6},{3,7},{4,0},{5,1},{6,2},{7,3},{8,12},{9,13},{10,... | collective-permute-start | bytes 1572872 | tf_op jit(solution)/shard_map/ppermute | solution.py:11
  25.8 3.7 copy-start.15
  25.8 28.5 %collective-permute-start = (bf16[2,128,1024]{2,1,0:T(8,128)(2,1)}, bf16[2,128,1024]{2,1,0:T(8,128)(2,1)}, u32[]{:S(2)}, u32[]{:S(2)}) collective-permute-start(bf16[2,128,1024]{2,1,0:T(8,128)(2,1)} %pad_maximum_fusion.3), channel_id=1, source_target_pairs={{0,1},{1,0},{2,3},{3,2},{4,5},{5,4},{6,7},{7,6},{8,9},{9,8},{10,11... | collective-permute-start | bytes 1572872 | tf_op jit(solution)/shard_map/ppermute | solution.py:11
  75.1 13.2 %copy-start.3 = (bf16[512,1024]{0,1:T(8,128)(2,1)S(1)}, bf16[512,1024]{0,1:T(8,128)(2,1)}, u32[]{:S(2)}) copy-start(bf16[512,1024]{0,1:T(8,128)(2,1)} %copy.29) | copy-start | bytes 3145732
  75.1 13.2 %copy-start.7 = (bf16[1,128,1024]{1,2,0:T(8,128)(2,1)S(1)}, bf16[1,128,1024]{1,2,0:T(8,128)(2,1)}, u32[]{:S(2)}) copy-start(bf16[1,128,1024]{1,2,0:T(8,128)(2,1)} %copy.32) | copy-start | bytes 786436
  75.1 13.2 %copy-start.8 = (bf16[1,128,1024]{1,2,0:T(8,128)(2,1)S(1)}, bf16[1,128,1024]{1,2,0:T(8,128)(2,1)}, u32[]{:S(2)}) copy-start(bf16[1,128,1024]{1,2,0:T(8,128)(2,1)} %copy.30) | copy-start | bytes 786436
  241.3 6.6 %copy-start.11 = (f32[896,16,64]{0,2,1:T(8,128)S(1)}, f32[896,16,64]{0,2,1:T(8,128)}, u32[]{:S(2)}) copy-start(f32[896,16,64]{0,2,1:T(8,128)} %get-tuple-element.93) | copy-start | bytes 11010052
  242.9 13.2 %collective-permute-start.3 = (bf16[2,128,1024]{1,2,0:T(8,128)(2,1)S(1)}, bf16[2,128,1024]{1,2,0:T(8,128)(2,1)S(1)}, u32[]{:S(2)}, u32[]{:S(2)}) collective-permute-start(bf16[2,128,1024]{1,2,0:T(8,128)(2,1)S(1)} %pad_maximum_fusion.6), channel_id=1, source_target_pairs={{0,1},{1,0},{2,3},{3,2},{4,5},{5,4},{6,7},{7,6},{8,9},{9,8},{10,11... | collective-permute-start | bytes 1572872 | tf_op jit(solution)/shard_map/ppermute | solution.py:11
  244.7 23.5 %collective-permute-start.4 = (bf16[2,128,1024]{1,2,0:T(8,128)(2,1)S(1)}, bf16[2,128,1024]{1,2,0:T(8,128)(2,1)S(1)}, u32[]{:S(2)}, u32[]{:S(2)}) collective-permute-start(bf16[2,128,1024]{1,2,0:T(8,128)(2,1)S(1)} %pad_maximum_fusion.7), channel_id=1, source_target_pairs={{0,2},{1,3},{2,0},{3,1},{4,6},{5,7},{6,4},{7,5},{8,10},{9,11},{10,... | collective-permute-start | bytes 1572872 | tf_op jit(solution)/shard_map/ppermute | solution.py:11
  244.8 24.9 %collective-permute-start.5 = (bf16[2,128,1024]{1,2,0:T(8,128)(2,1)S(1)}, bf16[2,128,1024]{1,2,0:T(8,128)(2,1)S(1)}, u32[]{:S(2)}, u32[]{:S(2)}) collective-permute-start(bf16[2,128,1024]{1,2,0:T(8,128)(2,1)S(1)} %pad_maximum_fusion.8), channel_id=1, source_target_pairs={{0,4},{1,5},{2,6},{3,7},{4,0},{5,1},{6,2},{7,3},{8,12},{9,13},{10,... | collective-permute-start | bytes 1572872 | tf_op jit(solution)/shard_map/ppermute | solution.py:11
  270.1 1.9 copy-start.4
  288.8 185.0 %all-gather.3.cloned.1.call-start = ((), (), s32[]{:S(2)}) async-start(), calls=%async_computation.1 | async-start | bytes 5242880 | tf_op jit(solution)/shard_map/all_gather | solution.py:144
  439.6 2.3 copy-start.13
  439.6 2.3 copy-start.21
  441.8 2.2 copy-start.14
  444.0 1.8 copy-start.2
  444.0 2.6 copy-start.10
  (6 other events, 8.6 us)
Sparse Core Ops, SparseCore 0:
  288.9 148.1 reduce-scatter.3
  439.7 34.0 all-gather.2
